TPU v7x, 128 devices: a whole 4x4x4 slice. The times are simulated.
128 devices in a mesh: tok: 16 (over x, y), wid: 8 (over z, core).
Axes of the slice: x: 4, y: 4, z: 4, core: 2. Of those that a mesh axis runs over, the one named last changes fastest.
Arguments:
- patches: bfloat16 [1536, 8, 6144], P('tok', None, 'wid'), may hold values from -6 to 6
- w_query: bfloat16 [6144, 4096], P('tok', 'wid'), may hold values from -0.102062073 to 0.102062073
- w_key: bfloat16 [6144, 4096], P('tok', 'wid'), may hold values from -0.102062073 to 0.102062073
- w_value: bfloat16 [6144, 4096], P('tok', 'wid'), may hold values from -0.078125 to 0.078125
- q_gain: float32 [4096], P('wid'), may hold values from 0.5 to 6
- k_gain: float32 [4096], P('wid'), may hold values from 0.5 to 6
- w_out: bfloat16 [4096, 6144], P('tok', 'wid'), may hold values from -0.09375 to 0.09375
Outputs:
- layer_out: bfloat16 [1536, 8, 6144], P('tok', None, 'wid')
All inputs are finite; a program needn't handle non-finite values.
Results may differ from a plain program's by a relative error of at most 0.0034.
The roundings to bfloat16 on the way count: a program that leaves them out, or rounds other values in their place, can miss the bound.
Values may be sent and summed in bfloat16 or wider, within the bound.
No kernel may reach another device: no remote copies, remote signals or barrier semaphores. Data moves between devices by JAX's collectives and lax.ppermute only.
A program may use at most 128 MiB of HBM per device.

v0:
```python
import jax
import jax.numpy as jnp
from jax import lax
from jax.sharding import PartitionSpec as P

D = 6144
HEAD_DIM = 128
HD = 4096


def layer_norm_rows(values, eps):
    mean = jnp.mean(values, axis=-1, keepdims=True)
    var = jnp.mean(values * values, axis=-1, keepdims=True) - mean * mean
    return (values - mean) * lax.rsqrt(var + eps)


def add_rows(left, piece):
    return jnp.dot(left, piece, preferred_element_type=jnp.float32)


def head_norm(values, gain, eps):
    rows, images, width = values.shape
    heads_here = width // HEAD_DIM
    shaped = values.reshape(rows, images, heads_here, HEAD_DIM)
    normed = layer_norm_rows(shaped, eps) * gain.reshape(heads_here, HEAD_DIM)
    return normed.astype(jnp.bfloat16).reshape(rows, images * heads_here, HEAD_DIM)


def local(patches, w_query, w_key, w_value, q_gain, k_gain, w_out):
    local_rows, images, local_width = patches.shape
    as_float = patches.astype(jnp.float32)
    totals = lax.psum((jnp.sum(as_float, axis=-1), jnp.sum(as_float * as_float, axis=-1)), "wid")
    mean = totals[0] / D
    var = totals[1] / D - mean * mean
    normed = ((as_float - mean[..., None]) * lax.rsqrt(var + 1e-06)[..., None]).astype(jnp.bfloat16)
    whole = lax.all_gather(normed, "wid", axis=2, tiled=True)
    flat = whole.reshape(local_rows * images, D)

    def add_one(piece):
        return add_rows(flat, piece)

    query = add_one(lax.all_gather(w_query, "tok", axis=0, tiled=True))
    key = add_one(lax.all_gather(w_key, "tok", axis=0, tiled=True))
    value = add_one(lax.all_gather(w_value, "tok", axis=0, tiled=True))
    head_width = query.shape[1]
    heads_here = head_width // HEAD_DIM
    qnorm = head_norm(query.reshape(local_rows, images, head_width), q_gain, 1e-06)
    knorm = head_norm(key.reshape(local_rows, images, head_width), k_gain, 1e-06)
    vshaped = value.astype(jnp.bfloat16).reshape(local_rows, images * heads_here, HEAD_DIM)
    qfull, kfull, vfull = (
        lax.all_to_all(qnorm, "tok", split_axis=1, concat_axis=0, tiled=True),
        lax.all_to_all(knorm, "tok", split_axis=1, concat_axis=0, tiled=True),
        lax.all_to_all(vshaped, "tok", split_axis=1, concat_axis=0, tiled=True),
    )
    seq_rows, item_count, _ = qfull.shape
    block = min(512, seq_rows)
    blocks = qfull.reshape(seq_rows // block, block, item_count, HEAD_DIM)
    scale = HEAD_DIM ** (-0.5)

    def attend(qblock):
        scores = (
            jnp.einsum("qid,kid->iqk", qblock, kfull, preferred_element_type=jnp.float32) * scale
        )
        top = jnp.max(scores, axis=-1, keepdims=True)
        expo = jnp.exp(scores - top)
        probs = (expo / jnp.sum(expo, axis=-1, keepdims=True)).astype(jnp.bfloat16)
        return jnp.einsum("iqk,kid->qid", probs, vfull, preferred_element_type=jnp.float32).astype(
            jnp.bfloat16
        )

    attended = lax.map(attend, blocks).reshape(seq_rows, item_count, HEAD_DIM)
    returned = lax.all_to_all(attended, "tok", split_axis=0, concat_axis=1, tiled=True)
    mixed = returned.reshape(local_rows, images, head_width)
    mixed_whole = lax.all_gather(mixed, "wid", axis=2, tiled=True).reshape(local_rows * images, HD)
    branch = add_rows(mixed_whole, lax.all_gather(w_out, "tok", axis=0, tiled=True))
    return (as_float + branch.reshape(local_rows, images, local_width)).astype(jnp.bfloat16)


def solution(mesh):
    placed = (
        P("tok", None, "wid"),
        P("tok", "wid"),
        P("tok", "wid"),
        P("tok", "wid"),
        P("wid"),
        P("wid"),
        P("tok", "wid"),
    )
    return jax.shard_map(
        local, mesh=mesh, in_specs=placed, out_specs=P("tok", None, "wid"), check_vma=False
    )
```

profile of v0, /device:TPU:1, one launch (start us, length us, event | category | flops | bytes accessed | tf_op | source)
XLA Modules:
  0.0 413.2 jit_solution(13096195138960030265)
XLA Ops:
  9.9 14.7 %all-reduce = (f32[96,8]{0,1:T(8,128)S(1)}, f32[96,8]{0,1:T(8,128)S(1)}) all-reduce(f32[96,8]{0,1:T(8,128)S(1)} %copy.64, f32[96,8]{0,1:T(8,128)S(1)} %copy.62), channel_id=1, replica_groups=mesh['tok'=16,'wid'=8] {'wid'}, use_global_device_ids=true, to_apply=%region_3.0 | all-reduce | flops 1536 | bytes 12288 | tf_op jit(solution)/shard_map/psum | solution.py:32
  28.6 45.1 %all-gather.11.cloned.1.call-done = bf16[6144,512]{1,0:T(8,128)(2,1)} async-done(((bf16[384,512]{1,0:T(8,128)(2,1)}), bf16[6144,512]{1,0:T(8,128)(2,1)}) %all-gather.11.cloned.1.call-update) | async-done | bytes 6291472 | tf_op jit(solution)/shard_map/all_gather | solution.py:43
  73.7 8.6 %copy.73 = bf16[512,6144]{1,0:T(8,128)(2,1)} copy(bf16[512,6144]{0,1:T(8,128)(2,1)} %bitcast.87) | data formatting | bytes 12582912 | tf_op jit(solution)/shard_map/dot_general | solution.py:18
  82.4 54.4 %all-gather.9.cloned.1.call-done = bf16[6144,512]{1,0:T(8,128)(2,1)} async-done(((bf16[384,512]{1,0:T(8,128)(2,1)}), bf16[6144,512]{1,0:T(8,128)(2,1)}) %all-gather.9.cloned.1.call-update) | async-done | bytes 6291472 | tf_op jit(solution)/shard_map/all_gather | solution.py:42
  136.8 8.7 %copy.66 = bf16[512,6144]{1,0:T(8,128)(2,1)} copy(bf16[512,6144]{0,1:T(8,128)(2,1)} %bitcast.88) | data formatting | bytes 12582912 | tf_op jit(solution)/shard_map/dot_general | solution.py:18
  145.5 47.6 %all-gather.7.cloned.1.call-done = bf16[96,8,6144]{2,1,0:T(8,128)(2,1)} async-done(((bf16[96,8,768]{2,1,0:T(8,128)(2,1)}), bf16[96,8,6144]{2,1,0:T(8,128)(2,1)}) %all-gather.7.cloned.1.call-update) | async-done | bytes 9437200 | tf_op jit(solution)/shard_map/all_gather | solution.py:36
  193.1 9.8 %fusion.44 = (f32[96,8,4]{1,2,0:T(4,128)S(1)}, f32[96,8,4]{1,2,0:T(4,128)S(1)}, f32[96,8,4,128]{3,1,2,0:T(8,128)S(1)}) fusion(bf16[4,128,6144,1]{2,1,0,3:T(8,128)(2,1)} %bitcast.90, bf16[96,8,6144]{2,1,0:T(8,128)(2,1)} %all-gather.7.cloned.1.call-done), kind=kOutput, calls=%fused_computation.46 | convolution fusion | flops 4833011712 | bytes 17326080 | tf_op jit(solution)/shard_map/dot_general | solution.py:18
  205.6 6.5 %all-to-all-start.1 = ((bf16[96,32,128]{2,0,1:T(8,128)(2,1)}), bf16[96,32,128]{2,0,1:T(8,128)(2,1)S(1)}, u32[]{:S(2)}, u32[]{:S(2)}) async-start(bf16[96,32,128]{2,0,1:T(8,128)(2,1)} %bitcast.18), calls=%async_computation.1 | async-start | bytes 1572864 | tf_op jit(solution)/shard_map/all_to_all | solution.py:52
  212.1 9.8 %fusion.45 = (f32[96,8,4]{1,2,0:T(4,128)S(1)}, f32[96,8,4]{1,2,0:T(4,128)S(1)}, f32[96,8,4,128]{3,1,2,0:T(8,128)S(1)}) fusion(bf16[4,128,6144,1]{2,1,0,3:T(8,128)(2,1)} %bitcast.89, bf16[96,8,6144]{2,1,0:T(8,128)(2,1)} %all-gather.7.cloned.1.call-done), kind=kOutput, calls=%fused_computation.47 | convolution fusion | flops 4833011712 | bytes 17326080 | tf_op jit(solution)/shard_map/dot_general | solution.py:18
  231.3 38.9 %all-gather.13.cloned.1.call-done = bf16[6144,512]{1,0:T(8,128)(2,1)} async-done(((bf16[384,512]{1,0:T(8,128)(2,1)}), bf16[6144,512]{1,0:T(8,128)(2,1)}) %all-gather.13.cloned.1.call-update) | async-done | bytes 6291472 | tf_op jit(solution)/shard_map/all_gather | solution.py:44
  270.2 9.9 %fusion.41 = bf16[768,512]{1,0:T(8,128)(2,1)S(1)} fusion(bf16[6144,512]{1,0:T(8,128)(2,1)} %all-gather.13.cloned.1.call-done, bf16[96,8,6144]{2,1,0:T(8,128)(2,1)} %all-gather.7.cloned.1.call-done), kind=kOutput, calls=%fused_computation.39 | convolution fusion | flops 4832231424 | bytes 16515072 | tf_op jit(solution)/shard_map/dot_general | solution.py:18
  281.8 4.3 %all-to-all-start.2 = ((bf16[96,32,128]{2,0,1:T(8,128)(2,1)}), bf16[96,32,128]{2,0,1:T(8,128)(2,1)S(1)}, u32[]{:S(2)}, u32[]{:S(2)}) async-start(bf16[96,32,128]{2,0,1:T(8,128)(2,1)} %copy.80), calls=%async_computation.2 | async-start | bytes 1572864 | tf_op jit(solution)/shard_map/all_to_all | solution.py:53
  286.2 14.3 %all-to-all-done.2 = bf16[96,32,128]{2,0,1:T(8,128)(2,1)S(1)} async-done(((bf16[96,32,128]{2,0,1:T(8,128)(2,1)}), bf16[96,32,128]{2,0,1:T(8,128)(2,1)S(1)}, u32[]{:S(2)}, u32[]{:S(2)}) %all-to-all-start.2) | async-done | bytes 786464 | tf_op jit(solution)/shard_map/all_to_all | solution.py:53
  300.6 27.7 %while.10 = (s32[]{:T(128)}, bf16[3,512,2,128]{3,1,0,2:T(8,128)(2,1)}, bf16[3,512,2,128]{3,1,0,2:T(8,128)(2,1)S(1)}, bf16[1536,2,128]{2,0,1:T(8,128)(2,1)S(1)}, bf16[1536,2,128]{2,0,1:T(8,128)(2,1)S(1)}, /*index=5*/s32[]{:T(128)}) while((s32[]{:T(128)}, bf16[3,512,2,128]{3,1,0,2:T(8,128)(2,1)}, bf16[3,512,2,128]{3,1,0,2:T(8,128)(2,1)S(1)}, ...), condition=%wide.region_11.12_spmd, body=%wide.region_8.11_spmd.sunk | while | flops 813303296 | bytes 14688841 | solution.py:71
  300.6 4.6 %fusion.66 = (f32[2,512]{1,0:T(2,128)S(1)}, f32[2,512,1536]{2,1,0:T(8,128)}) fusion(bf16[1536,2,128]{2,0,1:T(8,128)(2,1)S(1)} %get-tuple-element.136, bf16[3,512,2,128]{3,1,0,2:T(8,128)(2,1)S(1)} %get-tuple-element.135, s32[]{:T(128)} %get-tuple-element.127), kind=kOutput, calls=%fused_computation.48.clone.1 | convolution fusion | flops 407373312 | bytes 7344132 | tf_op jit(solution)/shard_map/while/body/eval_jaxpr/sub | solution.py:65
  305.2 4.5 %fusion.67 = bf16[3,512,2,128]{3,1,0,2:T(8,128)(2,1)} fusion(bf16[3,512,2,128]{3,1,0,2:T(8,128)(2,1)} %get-tuple-element.128, s32[]{:T(128)} %get-tuple-element.127, bf16[1536,2,128]{2,0,1:T(8,128)(2,1)S(1)} %get-tuple-element.137, f32[2,512,1536]{2,1,0:T(8,128)} %get-tuple-element.119, f32[2,512]{1,0:T(2,128)S(1)} %get-tuple-element.120), kind=kOutput, calls=%fused_computation.9.clone.1 | convolution fusion | flops 405929984 | bytes 7344640 | tf_op jit(solution)/shard_map/while/body/eval_jaxpr/iqk,kid->qid/dot_general | solution.py:67
  309.7 4.6 %fusion.66 = (f32[2,512]{1,0:T(2,128)S(1)}, f32[2,512,1536]{2,1,0:T(8,128)}) fusion(bf16[1536,2,128]{2,0,1:T(8,128)(2,1)S(1)} %get-tuple-element.136, bf16[3,512,2,128]{3,1,0,2:T(8,128)(2,1)S(1)} %get-tuple-element.135, s32[]{:T(128)} %get-tuple-element.127), kind=kOutput, calls=%fused_computation.48.clone.1 | convolution fusion | flops 407373312 | bytes 7344132 | tf_op jit(solution)/shard_map/while/body/eval_jaxpr/sub | solution.py:65
  314.4 4.6 %fusion.67 = bf16[3,512,2,128]{3,1,0,2:T(8,128)(2,1)} fusion(bf16[3,512,2,128]{3,1,0,2:T(8,128)(2,1)} %get-tuple-element.128, s32[]{:T(128)} %get-tuple-element.127, bf16[1536,2,128]{2,0,1:T(8,128)(2,1)S(1)} %get-tuple-element.137, f32[2,512,1536]{2,1,0:T(8,128)} %get-tuple-element.119, f32[2,512]{1,0:T(2,128)S(1)} %get-tuple-element.120), kind=kOutput, calls=%fused_computation.9.clone.1 | convolution fusion | flops 405929984 | bytes 7344640 | tf_op jit(solution)/shard_map/while/body/eval_jaxpr/iqk,kid->qid/dot_general | solution.py:67
  319.0 4.6 %fusion.66 = (f32[2,512]{1,0:T(2,128)S(1)}, f32[2,512,1536]{2,1,0:T(8,128)}) fusion(bf16[1536,2,128]{2,0,1:T(8,128)(2,1)S(1)} %get-tuple-element.136, bf16[3,512,2,128]{3,1,0,2:T(8,128)(2,1)S(1)} %get-tuple-element.135, s32[]{:T(128)} %get-tuple-element.127), kind=kOutput, calls=%fused_computation.48.clone.1 | convolution fusion | flops 407373312 | bytes 7344132 | tf_op jit(solution)/shard_map/while/body/eval_jaxpr/sub | solution.py:65
  323.6 4.6 %fusion.67 = bf16[3,512,2,128]{3,1,0,2:T(8,128)(2,1)} fusion(bf16[3,512,2,128]{3,1,0,2:T(8,128)(2,1)} %get-tuple-element.128, s32[]{:T(128)} %get-tuple-element.127, bf16[1536,2,128]{2,0,1:T(8,128)(2,1)S(1)} %get-tuple-element.137, f32[2,512,1536]{2,1,0:T(8,128)} %get-tuple-element.119, f32[2,512]{1,0:T(2,128)S(1)} %get-tuple-element.120), kind=kOutput, calls=%fused_computation.9.clone.1 | convolution fusion | flops 405929984 | bytes 7344640 | tf_op jit(solution)/shard_map/while/body/eval_jaxpr/iqk,kid->qid/dot_general | solution.py:67
  328.3 6.8 %copy.84 = bf16[1536,2,128]{2,1,0:T(2,128)(2,1)S(1)} copy(bf16[1536,2,128]{2,0,1:T(8,128)(2,1)} %bitcast.98) | data formatting | bytes 1572864 | tf_op jit(solution)/shard_map/reshape | solution.py:71
  335.1 18.8 %all_to_all.66 = bf16[1536,2,128]{2,1,0:T(2,128)(2,1)S(1)} all-to-all(bf16[1536,2,128]{2,1,0:T(2,128)(2,1)S(1)} %copy.84), channel_id=1, replica_groups=mesh['tok'=16,'wid'=8] {'tok'}, dimensions={0} | all-to-all | bytes 1572864 | tf_op jit(solution)/shard_map/all_to_all | solution.py:72
  356.1 40.5 %all-gather.15.cloned.1.call-done = bf16[96,8,4096]{2,1,0:T(8,128)(2,1)} async-done(((bf16[96,8,512]{2,1,0:T(8,128)(2,1)}), bf16[96,8,4096]{2,1,0:T(8,128)(2,1)}) %all-gather.15.cloned.1.call-update) | async-done | bytes 6291472 | tf_op jit(solution)/shard_map/all_gather | solution.py:74
  396.5 9.8 %fusion.38 = bf16[96,8,768]{2,1,0:T(8,128)(2,1)} fusion(bf16[96,8,768]{2,1,0:T(8,128)(2,1)S(1)} %copy-done, bf16[96,8,4096]{2,1,0:T(8,128)(2,1)} %all-gather.15.cloned.1.call-done, bf16[4096,768]{1,0:T(8,128)(2,1)} %all-gather.17.cloned.1.call-done), kind=kOutput, calls=%fused_computation.34 | convolution fusion | flops 4833607680 | bytes 14942208 | tf_op jit(solution)/shard_map/dot_general | solution.py:18
  (52 shorter events, 23.3 us)
Async XLA Ops:
  6.5 67.2 %all-gather.11.cloned.1.call-start = ((), (), s32[]{:S(2)}) async-start(), calls=%async_computation.6 | async-start | bytes 6684672 | tf_op jit(solution)/shard_map/all_gather | solution.py:43
  7.3 129.5 %all-gather.9.cloned.1.call-start = ((), (), s32[]{:S(2)}) async-start(), calls=%async_computation.5 | async-start | bytes 6684672 | tf_op jit(solution)/shard_map/all_gather | solution.py:42
  8.0 185.1 %all-gather.7.cloned.1.call-start = ((), (), s32[]{:S(2)}) async-start(), calls=%async_computation.4 | async-start | bytes 10616832 | tf_op jit(solution)/shard_map/all_gather | solution.py:36
  27.5 242.7 %all-gather.13.cloned.1.call-start = ((), (), s32[]{:S(2)}) async-start(), calls=%async_computation.7 | async-start | bytes 6684672 | tf_op jit(solution)/shard_map/all_gather | solution.py:44
  28.1 328.0 %all-gather.17.cloned.1.call-start = ((), (), s32[]{:S(2)}) async-start(), calls=%async_computation.9 | async-start | bytes 6684672 | tf_op jit(solution)/shard_map/all_gather | solution.py:75
  193.1 10.3 %copy-start.1 = (f32[512]{0:T(512)S(1)}, f32[512]{0:T(512)}, u32[]{:S(2)}) copy-start(f32[512]{0:T(512)} %param.14) | copy-start | bytes 6148
  205.6 21.5 %all-to-all-start.1 = ((bf16[96,32,128]{2,0,1:T(8,128)(2,1)}), bf16[96,32,128]{2,0,1:T(8,128)(2,1)S(1)}, u32[]{:S(2)}, u32[]{:S(2)}) async-start(bf16[96,32,128]{2,0,1:T(8,128)(2,1)} %bitcast.18), calls=%async_computation.1 | async-start | bytes 1572864 | tf_op jit(solution)/shard_map/all_to_all | solution.py:52
  212.1 10.3 %copy-start.2 = (f32[512]{0:T(512)S(1)}, f32[512]{0:T(512)}, u32[]{:S(2)}) copy-start(f32[512]{0:T(512)} %param.13) | copy-start | bytes 6148
  227.0 54.7 %all-to-all-start = ((bf16[96,32,128]{2,0,1:T(8,128)(2,1)}), bf16[96,32,128]{2,0,1:T(8,128)(2,1)S(1)}, u32[]{:S(2)}, u32[]{:S(2)}) async-start(bf16[96,32,128]{2,0,1:T(8,128)(2,1)} %bitcast.9), calls=%async_computation | async-start | bytes 1572864 | tf_op jit(solution)/shard_map/all_to_all | solution.py:51
  281.8 18.8 %all-to-all-start.2 = ((bf16[96,32,128]{2,0,1:T(8,128)(2,1)}), bf16[96,32,128]{2,0,1:T(8,128)(2,1)S(1)}, u32[]{:S(2)}, u32[]{:S(2)}) async-start(bf16[96,32,128]{2,0,1:T(8,128)(2,1)} %copy.80), calls=%async_computation.2 | async-start | bytes 1572864 | tf_op jit(solution)/shard_map/all_to_all | solution.py:53
  286.0 110.5 %all-gather.15.cloned.1.call-start = ((), (), s32[]{:S(2)}) async-start(), calls=%async_computation.8 | async-start | bytes 7077888 | tf_op jit(solution)/shard_map/all_gather | solution.py:74
  328.3 68.3 %copy-start = (bf16[96,8,768]{2,1,0:T(8,128)(2,1)S(1)}, bf16[96,8,768]{2,1,0:T(8,128)(2,1)}, u32[]{:S(2)}) copy-start(bf16[96,8,768]{2,1,0:T(8,128)(2,1)} %param.9) | copy-start | bytes 3538948
Sparse Core Ops, SparseCore 0:
  9.5 64.1 all-gather.10
  75.9 60.8 all-gather.8
  138.5 54.5 all-gather.6
  195.1 75.0 all-gather.12
  272.2 66.2 all-gather.16
  356.1 40.3 all-gather.14
where the time goes:
time: 414 us; the launch traced here: 413 us
  waiting for transfers between devices  246 us (59%)
  matrix products  66.9 us (16%)
  blocking collectives  33.5 us (8%)
  local copies, waits for them, and re-layouts  31.7 us (8%)
  starting transfers between devices  15.2 us (4%)
  between operations  13.7 us (3%)
  other arithmetic  6.42 us (2%)
    all_gather x1, waiting for transfers between devices, local(): query = add_one(lax.all_gather(w_query, 'tok', axis=0, tiled=True))  54.4 us
    all_gather x1, waiting for transfers between devices, local(): whole = lax.all_gather(normed, 'wid', axis=2, tiled=True)  47.6 us
    all_gather x1, waiting for transfers between devices, local(): key = add_one(lax.all_gather(w_key, 'tok', axis=0, tiled=True))  45.1 us
    all_gather x1, waiting for transfers between devices, local(): lax.all_gather(mixed, 'wid', axis=2, tiled=True)  40.5 us
    dot_general x4, matrix products, add_rows(): return jnp.dot(left, piece, preferred_element_type=jnp.float32)  39.2 us
    all_gather x1, waiting for transfers between devices, local(): value = add_one(lax.all_gather(w_value, 'tok', axis=0, tiled=True))  38.9 us
    all_to_all x1, blocking collectives, local(): lax.all_to_all(attended, 'tok', split_axis=0, concat_axis=1, tiled=True)  18.8 us
    dot_general x2, local copies, waits for them, and re-layouts, add_rows(): return jnp.dot(left, piece, preferred_element_type=jnp.float32)  17.4 us
  transfers between devices with their start and end apart: 9, of which 7 were waited for; matrix products, arithmetic and copies ran while one was open for 23% of the time, Pallas kernels for 0%

commit v1 on v0

--- a/solution.py
+++ b/solution.py
@@ -2,6 +2,7 @@
 import jax.numpy as jnp
 from jax import lax
 from jax.sharding import PartitionSpec as P
+from jax.lax import all_to_all, axis_size
 
 D = 6144
 HEAD_DIM = 128
@@ -47,9 +48,17 @@
     qnorm = head_norm(query.reshape(local_rows, images, head_width), q_gain, 1e-06)
     knorm = head_norm(key.reshape(local_rows, images, head_width), k_gain, 1e-06)
     vshaped = value.astype(jnp.bfloat16).reshape(local_rows, images * heads_here, HEAD_DIM)
+
+    def draft_islands_on_mesh(xx):
+        y = axis_size("tok")
+        passed = jnp.split(xx, y, axis=1)
+        aux = jnp.stack(passed)
+        z_new = all_to_all(aux, "tok", 0, 0)
+        return jnp.concatenate(z_new, 0)
+
     qfull, kfull, vfull = (
         lax.all_to_all(qnorm, "tok", split_axis=1, concat_axis=0, tiled=True),
-        lax.all_to_all(knorm, "tok", split_axis=1, concat_axis=0, tiled=True),
+        draft_islands_on_mesh(knorm),
         lax.all_to_all(vshaped, "tok", split_axis=1, concat_axis=0, tiled=True),
     )
     seq_rows, item_count, _ = qfull.shape

time: 414 us -> 434 us (1.048)
  local copies, waits for them, and re-layouts: 31.7 us -> 43.2 us
  waiting for transfers between devices: 246 us -> 256 us
    all_to_all x1, waiting for transfers between devices: 2.42 us -> 18.9 us  [draft_islands_on_mesh(): z_new = all_to_all(aux, 'tok', 0, 0)]
    unnamed x6 -> x21, local copies, waits for them, and re-layouts: 0.01 us -> 9.34 us
    all_gather x1, waiting for transfers between devices: 38.9 us -> 33.1 us  [local(): value = add_one(lax.all_gather(w_value, 'tok', axis=0, tiled=True))]
  transfers between devices with their start and end apart: 9 -> 9, of which waited for: 7 -> 7; matrix products, arithmetic and copies ran while one was open for 23% -> 25% of each run, Pallas kernels for 0% -> 0%
where the time goes in v1:
time: 434 us; the launch traced here: 433 us
  waiting for transfers between devices  256 us (59%)
  matrix products  64.8 us (15%)
  local copies, waits for them, and re-layouts  43.2 us (10%)
  blocking collectives  32 us (7%)
  starting transfers between devices  15.2 us (4%)
  between operations  13.7 us (3%)
  other arithmetic  8.4 us (2%)
    all_gather x1, waiting for transfers between devices, local(): query = add_one(lax.all_gather(w_query, 'tok', axis=0, tiled=True))  54.4 us
    all_gather x1, waiting for transfers between devices, local(): whole = lax.all_gather(normed, 'wid', axis=2, tiled=True)  47.6 us
    all_gather x1, waiting for transfers between devices, local(): key = add_one(lax.all_gather(w_key, 'tok', axis=0, tiled=True))  45.1 us
    all_gather x1, waiting for transfers between devices, local(): lax.all_gather(mixed, 'wid', axis=2, tiled=True)  41.2 us
    dot_general x4, matrix products, add_rows(): return jnp.dot(left, piece, preferred_element_type=jnp.float32)  37.3 us
    all_gather x1, waiting for transfers between devices, local(): value = add_one(lax.all_gather(w_value, 'tok', axis=0, tiled=True))  33.1 us
    all_to_all x1, waiting for transfers between devices, draft_islands_on_mesh(): z_new = all_to_all(aux, 'tok', 0, 0)  18.9 us
    dot_general x2, local copies, waits for them, and re-layouts, add_rows(): return jnp.dot(left, piece, preferred_element_type=jnp.float32)  17.4 us
  transfers between devices with their start and end apart: 9, of which 7 were waited for; matrix products, arithmetic and copies ran while one was open for 25% of the time, Pallas kernels for 0%

profile of v1, /device:TPU:1, one launch (start us, length us, event | category | flops | bytes accessed | tf_op | source)
XLA Modules:
  0.0 432.9 jit_solution(12036060431801987641)
XLA Ops:
  9.9 14.7 %all-reduce = (f32[96,8]{0,1:T(8,128)S(1)}, f32[96,8]{0,1:T(8,128)S(1)}) all-reduce(f32[96,8]{0,1:T(8,128)S(1)} %copy.79, f32[96,8]{0,1:T(8,128)S(1)} %copy.77), channel_id=1, replica_groups=mesh['tok'=16,'wid'=8] {'wid'}, use_global_device_ids=true, to_apply=%region_3.0 | all-reduce | flops 1536 | bytes 12288 | tf_op jit(solution)/shard_map/psum | solution.py:33
  28.6 45.1 %all-gather.11.cloned.1.call-done = bf16[6144,512]{1,0:T(8,128)(2,1)} async-done(((bf16[384,512]{1,0:T(8,128)(2,1)}), bf16[6144,512]{1,0:T(8,128)(2,1)}) %all-gather.11.cloned.1.call-update) | async-done | bytes 6291472 | tf_op jit(solution)/shard_map/all_gather | solution.py:44
  73.7 8.6 %copy.88 = bf16[512,6144]{1,0:T(8,128)(2,1)} copy(bf16[512,6144]{0,1:T(8,128)(2,1)} %bitcast.148) | data formatting | bytes 12582912 | tf_op jit(solution)/shard_map/dot_general | solution.py:19
  82.4 54.4 %all-gather.9.cloned.1.call-done = bf16[6144,512]{1,0:T(8,128)(2,1)} async-done(((bf16[384,512]{1,0:T(8,128)(2,1)}), bf16[6144,512]{1,0:T(8,128)(2,1)}) %all-gather.9.cloned.1.call-update) | async-done | bytes 6291472 | tf_op jit(solution)/shard_map/all_gather | solution.py:43
  136.8 8.7 %copy.81 = bf16[512,6144]{1,0:T(8,128)(2,1)} copy(bf16[512,6144]{0,1:T(8,128)(2,1)} %bitcast.149) | data formatting | bytes 12582912 | tf_op jit(solution)/shard_map/dot_general | solution.py:19
  145.5 47.6 %all-gather.7.cloned.1.call-done = bf16[96,8,6144]{2,1,0:T(8,128)(2,1)} async-done(((bf16[96,8,768]{2,1,0:T(8,128)(2,1)}), bf16[96,8,6144]{2,1,0:T(8,128)(2,1)}) %all-gather.7.cloned.1.call-update) | async-done | bytes 9437200 | tf_op jit(solution)/shard_map/all_gather | solution.py:37
  193.1 10.7 %fusion.60 = (f32[96,8,4]{1,2,0:T(4,128)S(1)}, f32[96,8,4]{1,2,0:T(4,128)S(1)}, f32[96,8,4,128]{3,1,2,0:T(8,128)S(1)}) fusion(bf16[4,128,6144,1]{2,1,0,3:T(8,128)(2,1)} %bitcast.150, bf16[96,8,6144]{2,1,0:T(8,128)(2,1)} %all-gather.7.cloned.1.call-done), kind=kOutput, calls=%fused_computation.78 | convolution fusion | flops 4833011712 | bytes 17326080 | tf_op jit(solution)/shard_map/dot_general | solution.py:19
  203.8 6.9 %fusion.61 = (f32[96,8,4]{1,2,0:T(4,128)}, f32[96,8,4]{1,2,0:T(4,128)}, f32[96,8,4,128]{3,1,2,0:T(8,128)S(1)}) fusion(bf16[4,128,6144,1]{2,1,0,3:T(8,128)(2,1)S(1)} %bitcast.151, bf16[96,8,6144]{2,1,0:T(8,128)(2,1)S(1)} %copy-done.2), kind=kOutput, calls=%fused_computation.79 | convolution fusion | flops 4833011712 | bytes 17326080 | tf_op jit(solution)/shard_map/dot_general | solution.py:19
  219.7 6.5 %all-to-all-start = ((bf16[96,32,128]{2,0,1:T(8,128)(2,1)}), bf16[96,32,128]{2,0,1:T(8,128)(2,1)S(1)}, u32[]{:S(2)}, u32[]{:S(2)}) async-start(bf16[96,32,128]{2,0,1:T(8,128)(2,1)} %bitcast.9), calls=%async_computation | async-start | bytes 1572864 | tf_op jit(solution)/shard_map/all_to_all | solution.py:60
  231.2 33.1 %all-gather.13.cloned.1.call-done = bf16[6144,512]{1,0:T(8,128)(2,1)} async-done(((bf16[384,512]{1,0:T(8,128)(2,1)}), bf16[6144,512]{1,0:T(8,128)(2,1)}) %all-gather.13.cloned.1.call-update) | async-done | bytes 6291472 | tf_op jit(solution)/shard_map/all_gather | solution.py:45
  264.3 9.9 %fusion.41 = bf16[768,512]{1,0:T(8,128)(2,1)S(1)} fusion(bf16[6144,512]{1,0:T(8,128)(2,1)} %all-gather.13.cloned.1.call-done, bf16[96,8,6144]{2,1,0:T(8,128)(2,1)} %all-gather.7.cloned.1.call-done), kind=kOutput, calls=%fused_computation.39 | convolution fusion | flops 4832231424 | bytes 16515072 | tf_op jit(solution)/shard_map/dot_general | solution.py:19
  278.3 4.8 %all-to-all-start.2 = ((bf16[96,32,128]{2,0,1:T(8,128)(2,1)}), bf16[96,32,128]{2,0,1:T(8,128)(2,1)S(1)}, u32[]{:S(2)}, u32[]{:S(2)}) async-start(bf16[96,32,128]{2,0,1:T(8,128)(2,1)} %copy.95), calls=%async_computation.2 | async-start | bytes 1572864 | tf_op jit(solution)/shard_map/all_to_all | solution.py:62
  285.7 12.8 %all-to-all-done.2 = bf16[96,32,128]{2,0,1:T(8,128)(2,1)S(1)} async-done(((bf16[96,32,128]{2,0,1:T(8,128)(2,1)}), bf16[96,32,128]{2,0,1:T(8,128)(2,1)S(1)}, u32[]{:S(2)}, u32[]{:S(2)}) %all-to-all-start.2) | async-done | bytes 786464 | tf_op jit(solution)/shard_map/all_to_all | solution.py:62
  302.3 18.9 %all-to-all-done.1 = bf16[16,96,2,128]{3,1,2,0:T(8,128)(2,1)S(1)} async-done(((bf16[16,96,2,128]{3,1,2,0:T(8,128)(2,1)}), bf16[16,96,2,128]{3,1,2,0:T(8,128)(2,1)S(1)}, u32[]{:S(2)}, u32[]{:S(2)}) %all-to-all-start.1) | async-done | bytes 786464 | tf_op jit(solution)/shard_map/all_to_all | solution.py:56
  321.3 27.6 %while.10 = (s32[]{:T(128)}, bf16[3,512,2,128]{3,1,0,2:T(8,128)(2,1)}, bf16[3,512,2,128]{3,1,0,2:T(8,128)(2,1)S(1)}, bf16[1536,2,128]{2,0,1:T(8,128)(2,1)S(1)}, bf16[1536,2,128]{2,0,1:T(8,128)(2,1)S(1)}, /*index=5*/s32[]{:T(128)}) while((s32[]{:T(128)}, bf16[3,512,2,128]{3,1,0,2:T(8,128)(2,1)}, bf16[3,512,2,128]{3,1,0,2:T(8,128)(2,1)S(1)}, ...), condition=%wide.region_11.12_spmd, body=%wide.region_8.11_spmd.sunk | while | flops 813303296 | bytes 14688841 | solution.py:80
  321.3 4.6 %fusion.82 = (f32[2,512]{1,0:T(2,128)S(1)}, f32[2,512,1536]{2,1,0:T(8,128)}) fusion(bf16[1536,2,128]{2,0,1:T(8,128)(2,1)S(1)} %get-tuple-element.136, bf16[3,512,2,128]{3,1,0,2:T(8,128)(2,1)S(1)} %get-tuple-element.135, s32[]{:T(128)} %get-tuple-element.127), kind=kOutput, calls=%fused_computation.80.clone.1 | convolution fusion | flops 407373312 | bytes 7344132 | tf_op jit(solution)/shard_map/while/body/eval_jaxpr/sub | solution.py:74
  325.9 4.6 %fusion.83 = bf16[3,512,2,128]{3,1,0,2:T(8,128)(2,1)} fusion(bf16[3,512,2,128]{3,1,0,2:T(8,128)(2,1)} %get-tuple-element.128, s32[]{:T(128)} %get-tuple-element.127, bf16[1536,2,128]{2,0,1:T(8,128)(2,1)S(1)} %get-tuple-element.137, f32[2,512,1536]{2,1,0:T(8,128)} %get-tuple-element.119, f32[2,512]{1,0:T(2,128)S(1)} %get-tuple-element.120), kind=kOutput, calls=%fused_computation.9.clone.1 | convolution fusion | flops 405929984 | bytes 7344640 | tf_op jit(solution)/shard_map/while/body/eval_jaxpr/iqk,kid->qid/dot_general | solution.py:76
  330.6 4.6 %fusion.82 = (f32[2,512]{1,0:T(2,128)S(1)}, f32[2,512,1536]{2,1,0:T(8,128)}) fusion(bf16[1536,2,128]{2,0,1:T(8,128)(2,1)S(1)} %get-tuple-element.136, bf16[3,512,2,128]{3,1,0,2:T(8,128)(2,1)S(1)} %get-tuple-element.135, s32[]{:T(128)} %get-tuple-element.127), kind=kOutput, calls=%fused_computation.80.clone.1 | convolution fusion | flops 407373312 | bytes 7344132 | tf_op jit(solution)/shard_map/while/body/eval_jaxpr/sub | solution.py:74
  339.7 4.6 %fusion.82 = (f32[2,512]{1,0:T(2,128)S(1)}, f32[2,512,1536]{2,1,0:T(8,128)}) fusion(bf16[1536,2,128]{2,0,1:T(8,128)(2,1)S(1)} %get-tuple-element.136, bf16[3,512,2,128]{3,1,0,2:T(8,128)(2,1)S(1)} %get-tuple-element.135, s32[]{:T(128)} %get-tuple-element.127), kind=kOutput, calls=%fused_computation.80.clone.1 | convolution fusion | flops 407373312 | bytes 7344132 | tf_op jit(solution)/shard_map/while/body/eval_jaxpr/sub | solution.py:74
  344.3 4.5 %fusion.83 = bf16[3,512,2,128]{3,1,0,2:T(8,128)(2,1)} fusion(bf16[3,512,2,128]{3,1,0,2:T(8,128)(2,1)} %get-tuple-element.128, s32[]{:T(128)} %get-tuple-element.127, bf16[1536,2,128]{2,0,1:T(8,128)(2,1)S(1)} %get-tuple-element.137, f32[2,512,1536]{2,1,0:T(8,128)} %get-tuple-element.119, f32[2,512]{1,0:T(2,128)S(1)} %get-tuple-element.120), kind=kOutput, calls=%fused_computation.9.clone.1 | convolution fusion | flops 405929984 | bytes 7344640 | tf_op jit(solution)/shard_map/while/body/eval_jaxpr/iqk,kid->qid/dot_general | solution.py:76
  348.8 6.8 %copy.99 = bf16[1536,2,128]{2,1,0:T(2,128)(2,1)S(1)} copy(bf16[1536,2,128]{2,0,1:T(8,128)(2,1)} %bitcast.40) | data formatting | bytes 1572864 | tf_op jit(solution)/shard_map/reshape | solution.py:80
  355.6 17.3 %all_to_all.53 = bf16[1536,2,128]{2,1,0:T(2,128)(2,1)S(1)} all-to-all(bf16[1536,2,128]{2,1,0:T(2,128)(2,1)S(1)} %copy.99), channel_id=1, replica_groups=mesh['tok'=16,'wid'=8] {'tok'}, dimensions={0} | all-to-all | bytes 1572864 | tf_op jit(solution)/shard_map/all_to_all | solution.py:81
  375.1 41.2 %all-gather.15.cloned.1.call-done = bf16[96,8,4096]{2,1,0:T(8,128)(2,1)} async-done(((bf16[96,8,512]{2,1,0:T(8,128)(2,1)}), bf16[96,8,4096]{2,1,0:T(8,128)(2,1)}) %all-gather.15.cloned.1.call-update) | async-done | bytes 6291472 | tf_op jit(solution)/shard_map/all_gather | solution.py:83
  416.2 9.8 %fusion.38 = bf16[96,8,768]{2,1,0:T(8,128)(2,1)} fusion(bf16[96,8,768]{2,1,0:T(8,128)(2,1)S(1)} %copy-done.1, bf16[96,8,4096]{2,1,0:T(8,128)(2,1)} %all-gather.15.cloned.1.call-done, bf16[4096,768]{1,0:T(8,128)(2,1)} %all-gather.17.cloned.1.call-done), kind=kOutput, calls=%fused_computation.34 | convolution fusion | flops 4833607680 | bytes 14942208 | tf_op jit(solution)/shard_map/dot_general | solution.py:19
  (68 shorter events, 38.3 us)
Async XLA Ops:
  6.5 67.2 %all-gather.11.cloned.1.call-start = ((), (), s32[]{:S(2)}) async-start(), calls=%async_computation.6 | async-start | bytes 6684672 | tf_op jit(solution)/shard_map/all_gather | solution.py:44
  7.3 129.5 %all-gather.9.cloned.1.call-start = ((), (), s32[]{:S(2)}) async-start(), calls=%async_computation.5 | async-start | bytes 6684672 | tf_op jit(solution)/shard_map/all_gather | solution.py:43
  8.0 185.1 %all-gather.7.cloned.1.call-start = ((), (), s32[]{:S(2)}) async-start(), calls=%async_computation.4 | async-start | bytes 10616832 | tf_op jit(solution)/shard_map/all_gather | solution.py:37
  27.5 236.8 %all-gather.13.cloned.1.call-start = ((), (), s32[]{:S(2)}) async-start(), calls=%async_computation.7 | async-start | bytes 6684672 | tf_op jit(solution)/shard_map/all_gather | solution.py:45
  28.1 347.0 %all-gather.17.cloned.1.call-start = ((), (), s32[]{:S(2)}) async-start(), calls=%async_computation.9 | async-start | bytes 6684672 | tf_op jit(solution)/shard_map/all_gather | solution.py:84
  193.1 10.7 %copy-start = (bf16[512,6144]{1,0:T(8,128)(2,1)S(1)}, bf16[512,6144]{1,0:T(8,128)(2,1)}, u32[]{:S(2)}) copy-start(bf16[512,6144]{1,0:T(8,128)(2,1)} %copy.81) | copy-start | bytes 18874372
  193.1 10.7 %copy-start.2 = (bf16[96,8,6144]{2,1,0:T(8,128)(2,1)S(1)}, bf16[96,8,6144]{2,1,0:T(8,128)(2,1)}, u32[]{:S(2)}) copy-start(bf16[96,8,6144]{2,1,0:T(8,128)(2,1)} %all-gather.7.cloned.1.call-done) | copy-start | bytes 28311556
  219.7 58.7 %all-to-all-start = ((bf16[96,32,128]{2,0,1:T(8,128)(2,1)}), bf16[96,32,128]{2,0,1:T(8,128)(2,1)S(1)}, u32[]{:S(2)}, u32[]{:S(2)}) async-start(bf16[96,32,128]{2,0,1:T(8,128)(2,1)} %bitcast.9), calls=%async_computation | async-start | bytes 1572864 | tf_op jit(solution)/shard_map/all_to_all | solution.py:60
  278.3 20.1 %all-to-all-start.2 = ((bf16[96,32,128]{2,0,1:T(8,128)(2,1)}), bf16[96,32,128]{2,0,1:T(8,128)(2,1)S(1)}, u32[]{:S(2)}, u32[]{:S(2)}) async-start(bf16[96,32,128]{2,0,1:T(8,128)(2,1)} %copy.95), calls=%async_computation.2 | async-start | bytes 1572864 | tf_op jit(solution)/shard_map/all_to_all | solution.py:62
  298.5 22.8 %all-to-all-start.1 = ((bf16[16,96,2,128]{3,1,2,0:T(8,128)(2,1)}), bf16[16,96,2,128]{3,1,2,0:T(8,128)(2,1)S(1)}, u32[]{:S(2)}, u32[]{:S(2)}) async-start(bf16[16,96,2,128]{3,1,2,0:T(8,128)(2,1)} %fusion.44), calls=%async_computation.1 | async-start | bytes 1572864 | tf_op jit(solution)/shard_map/all_to_all | solution.py:56
  302.1 114.2 %all-gather.15.cloned.1.call-start = ((), (), s32[]{:S(2)}) async-start(), calls=%async_computation.8 | async-start | bytes 7077888 | tf_op jit(solution)/shard_map/all_gather | solution.py:83
  348.8 67.4 %copy-start.1 = (bf16[96,8,768]{2,1,0:T(8,128)(2,1)S(1)}, bf16[96,8,768]{2,1,0:T(8,128)(2,1)}, u32[]{:S(2)}) copy-start(bf16[96,8,768]{2,1,0:T(8,128)(2,1)} %param.9) | copy-start | bytes 3538948
Sparse Core Ops, SparseCore 0:
  9.5 64.1 all-gather.10
  75.9 60.8 all-gather.8
  138.5 54.5 all-gather.6
  195.1 69.1 all-gather.12
  266.3 73.0 all-gather.16
  375.2 41.0 all-gather.14
